TPU v7x, 32 devices: a whole 2x2x4 slice. The times are simulated.
32 devices in a mesh: ctx: 8 (over z, x), dp: 4 (over y, core).
Axes of the slice: x: 2, y: 2, z: 4, core: 2. Of those that a mesh axis runs over, the one named last changes fastest.
Arguments:
- queries: bfloat16 [4, 2048, 512], P('dp', 'ctx'), may hold values from -3 to 3
- keys: bfloat16 [4, 2048, 512], P('dp', 'ctx'), may hold values from -6 to 6
- values: bfloat16 [4, 2048, 512], P('dp', 'ctx'), may hold values from -6 to 6
- gates: bfloat16 [4, 2048, 512], P('dp', 'ctx'), may hold values from -6 to 6
- out_grad: bfloat16 [4, 2048, 512], P('dp', 'ctx'), may hold values from -6 to 6
- time_bucket: int32 [4, 2048], P('dp'), may hold values from 0 to 127
- lengths: int32 [4, 6], P('dp'), may hold values from 1 to 1024, 2048 in all within a row
- block_map: int32 [4, 16, 16], P('dp'), may hold values 0 or 1
- bucket_bias_matrix: bfloat16 [4, 128, 128], replicated, may hold values from 1 to 3
- w_out: bfloat16 [512, 512], replicated, may hold values from -0.25 to 0.25
Outputs:
- query_grad: bfloat16 [4, 2048, 512], P('dp', 'ctx')
- key_grad: bfloat16 [4, 2048, 512], P('dp', 'ctx')
- value_grad: bfloat16 [4, 2048, 512], P('dp', 'ctx')
- gate_grad: bfloat16 [4, 2048, 512], P('dp', 'ctx')
- w_out_grad: float32 [512, 512], P('dp')
- table_grad: float32 [4, 128, 128], replicated
Inputs may be any that keep to these rules, and one draw needn't show every extreme that they name: Each row of lengths sums to 2048, and its largest entry is 1024. `block_map`: 1 marks a visible pair of blocks.
All inputs are finite; a program needn't handle non-finite values.
Results may differ from a plain program's by a relative error of at most 0.0059.
Values may be sent and summed in bfloat16 or wider, within the bound.
No kernel may reach another device: no remote copies, remote signals or barrier semaphores. Data moves between devices by JAX's collectives and lax.ppermute only.
A program may use at most 64 MiB of HBM per device.

v0:
```python
import jax
import jax.numpy as jnp
from jax import lax
from jax.sharding import PartitionSpec as P

BLK = 128
NORM_EPSILON = 1e-05


def passed_along(value, axis, by):
    length = lax.axis_size(axis)
    pairs = [(i, i + by) for i in range(length) if 0 <= i + by < length]
    return lax.ppermute(value, axis, pairs)


def silu_slope(scores):
    sigmoid = jax.nn.sigmoid(scores)
    return sigmoid * (1.0 + scores * (1.0 - sigmoid))


def expand_blocks(block_rows, block_size):
    return jnp.repeat(jnp.repeat(block_rows, block_size, axis=0), block_size, axis=1)


def shards(
    queries,
    keys,
    values,
    gates,
    out_grad,
    time_bucket,
    lengths,
    block_map,
    bucket_bias_matrix,
    w_out,
):
    query_rows = queries[0]
    key_rows = keys[0]
    value_rows = values[0]
    gate_rows = gates[0]
    grad_rows = out_grad[0]
    local_rows, width = query_rows.shape
    head_count = bucket_bias_matrix.shape[0]
    bucket_count = bucket_bias_matrix.shape[1]
    head_dim = width // head_count
    scale = head_dim ** (-0.5)
    blocks_here = local_rows // BLK
    cycle_index = lax.axis_index("ctx")
    row_start = cycle_index * local_rows
    offsets = jnp.cumsum(lengths[0], dtype=jnp.int32) - lengths[0]

    def segment_of(positions):
        return jnp.sum(
            (positions[:, None] >= offsets[None, 1:]).astype(jnp.int32), axis=1, dtype=jnp.int32
        )

    bucket_ids = jnp.arange(bucket_count, dtype=jnp.int32)
    query_pos = row_start + jnp.arange(local_rows, dtype=jnp.int32)
    query_seg = segment_of(query_pos)
    query_bucket = lax.dynamic_slice_in_dim(time_bucket[0], row_start, local_rows, 0)
    query_bucket_indicator = (query_bucket[:, None] == bucket_ids[None, :]).astype(jnp.bfloat16)
    bias_matrix_rows = jnp.einsum(
        "lf,sfq->slq",
        query_bucket_indicator,
        bucket_bias_matrix,
        preferred_element_type=jnp.float32,
    ).astype(jnp.bfloat16)
    map_rows = lax.dynamic_slice_in_dim(block_map[0], cycle_index * blocks_here, blocks_here, 0)
    query_heads = query_rows.reshape(local_rows, head_count, head_dim)
    stacked = jnp.stack([key_rows, value_rows])
    window = [stacked, passed_along(stacked, "ctx", 1), passed_along(stacked, "ctx", 2)]
    tiles = []
    attended = jnp.zeros((local_rows, head_count, head_dim), jnp.float32)
    for distance in range(3):
        key_first = row_start - distance * local_rows
        key_pos = key_first + jnp.arange(local_rows, dtype=jnp.int32)
        safe_first = jnp.maximum(key_first, 0)
        key_bucket = lax.dynamic_slice_in_dim(time_bucket[0], safe_first, local_rows, 0)
        key_bucket_indicator = (key_bucket[:, None] == bucket_ids[None, :]).astype(jnp.bfloat16)
        map_cols = lax.dynamic_slice_in_dim(map_rows, safe_first // BLK, blocks_here, 1)
        same_block = query_pos[:, None] // BLK == key_pos[None, :] // BLK
        key_visible = (
            (query_seg[:, None] == segment_of(key_pos)[None, :])
            & (key_pos[None, :] <= query_pos[:, None])
            & (key_pos[None, :] >= 0)
            & ((expand_blocks(map_cols, BLK) == 1) | same_block)
        )
        key_bias_terms = jnp.einsum(
            "vqx,px->vqp",
            bias_matrix_rows,
            key_bucket_indicator,
            preferred_element_type=jnp.float32,
        )
        visible, bias_terms, key_bucket_indicator = (
            key_visible,
            key_bias_terms,
            key_bucket_indicator,
        )
        forward_pair = window[distance]
        forward_key_heads = forward_pair[0].reshape(local_rows, head_count, head_dim)
        forward_value_heads = forward_pair[1].reshape(local_rows, head_count, head_dim)
        forward_scores = (
            jnp.einsum(
                "ihd,jhd->hij", query_heads, forward_key_heads, preferred_element_type=jnp.float32
            )
            * scale
            + bias_terms
        )
        forward_weights = jnp.where(visible[None], jax.nn.silu(forward_scores), 0.0).astype(
            jnp.bfloat16
        )
        attended_part = jnp.einsum(
            "hij,jhd->ihd", forward_weights, forward_value_heads, preferred_element_type=jnp.float32
        )
        attended = attended + attended_part
        tiles.append((visible, forward_scores, forward_weights, key_bucket_indicator))
    attended = attended.reshape(local_rows, width)
    centered = attended - jnp.mean(attended, axis=1, keepdims=True)
    inverse = lax.rsqrt(jnp.mean(centered * centered, axis=1, keepdims=True) + NORM_EPSILON)
    normed = centered * inverse
    dz_rows = lax.dot_general(
        grad_rows, w_out, (((1,), (1,)), ((), ())), preferred_element_type=jnp.float32
    )
    gate_float = gate_rows.astype(jnp.float32)
    gate_grad = (dz_rows * normed).astype(jnp.bfloat16)
    mixed = (normed * gate_float).astype(jnp.bfloat16)
    lifted = dz_rows * gate_float
    attended_grad = (
        (
            lifted
            - jnp.mean(lifted, axis=1, keepdims=True)
            - normed * jnp.mean(lifted * normed, axis=1, keepdims=True)
        )
        * inverse
    ).astype(jnp.bfloat16)
    grad_heads = attended_grad.reshape(local_rows, head_count, head_dim)
    indicator_float = query_bucket_indicator.astype(jnp.float32)
    query_sum = jnp.zeros((local_rows, width), jnp.float32)
    table_local = jnp.zeros((head_count, bucket_count, bucket_count), jnp.float32)
    key_terms = []
    for distance in range(3):
        visible, scores, weights, key_bucket_indicator = tiles[distance]
        pair = window[distance]
        key_heads = pair[0].reshape(local_rows, head_count, head_dim)
        value_heads = pair[1].reshape(local_rows, head_count, head_dim)
        weight_grad = jnp.einsum(
            "ihd,jhd->hij", grad_heads, value_heads, preferred_element_type=jnp.float32
        )
        value_part = jnp.einsum(
            "hij,ihd->jhd", weights, grad_heads, preferred_element_type=jnp.float32
        ).reshape(local_rows, width)
        score_gradient = jnp.where(visible[None], weight_grad * silu_slope(scores), 0.0).astype(
            jnp.bfloat16
        )
        query_part = jnp.einsum(
            "hij,jhd->ihd", score_gradient, key_heads, preferred_element_type=jnp.float32
        ).reshape(local_rows, width)
        key_part = (
            jnp.einsum(
                "hij,ihd->jhd", score_gradient, query_heads, preferred_element_type=jnp.float32
            ).reshape(local_rows, width)
            * scale
        )
        bucket_share_piece = jnp.einsum(
            "rmw,wx->rmx", score_gradient, key_bucket_indicator, preferred_element_type=jnp.float32
        )
        table_part = jnp.einsum(
            "qp,cqk->cpk", indicator_float, bucket_share_piece, precision=lax.Precision.HIGHEST
        )
        query_sum = query_sum + query_part
        table_local = table_local + table_part
        key_terms.append(jnp.stack([key_part, value_part]))
    gathered = (
        key_terms[0] + passed_along(key_terms[1], "ctx", -1) + passed_along(key_terms[2], "ctx", -2)
    )
    query_grad = (query_sum * scale).astype(jnp.bfloat16)
    key_grad = gathered[0].astype(jnp.bfloat16)
    value_grad = gathered[1].astype(jnp.bfloat16)
    weight_rows = lax.psum_scatter(
        lax.dot_general(
            mixed, grad_rows, (((0,), (0,)), ((), ())), preferred_element_type=jnp.float32
        ),
        "dp",
        scatter_dimension=0,
        tiled=True,
    )
    projection_grad = lax.psum(weight_rows, "ctx")
    table_grad = lax.psum(table_local, ("ctx", "dp"))
    return (
        query_grad[None],
        key_grad[None],
        value_grad[None],
        gate_grad[None],
        projection_grad,
        table_grad,
    )


def solution(mesh):
    return jax.shard_map(
        shards,
        mesh=mesh,
        in_specs=(
            P("dp", "ctx", None),
            P("dp", "ctx", None),
            P("dp", "ctx", None),
            P("dp", "ctx", None),
            P("dp", "ctx", None),
            P("dp", None),
            P("dp", None),
            P("dp", None, None),
            P(),
            P(),
        ),
        out_specs=(
            P("dp", "ctx", None),
            P("dp", "ctx", None),
            P("dp", "ctx", None),
            P("dp", "ctx", None),
            P("dp", None),
            P(),
        ),
        check_vma=False,
    )
```

profile of v0, /device:TPU:0, one launch (start us, length us, event | category | flops | bytes accessed | tf_op | source)
XLA Modules:
  0.0 265.2 jit_solution(2168080147234761298)
XLA Ops:
  8.1 1.2 copy.148
  9.4 0.9 pad_maximum_fusion.2
  10.2 5.8 %collective-permute-start.1 = (bf16[2,256,512]{1,2,0:T(8,128)(2,1)}, bf16[2,256,512]{1,2,0:T(8,128)(2,1)}, u32[]{:S(2)}, u32[]{:S(2)}) collective-permute-start(bf16[2,256,512]{1,2,0:T(8,128)(2,1)} %pad_maximum_fusion.2), channel_id=1, source_target_pairs={{0,8},{4,12},{8,16},{12,20},{16,24},{20,28},{1,9},{5,13},{9,17},{1... | collective-permute-start | bytes 1572872 | tf_op jit(solution)/shard_map/ppermute | solution.py:13
  16.0 4.2 %collective-permute-start = (bf16[2,256,512]{1,2,0:T(8,128)(2,1)}, bf16[2,256,512]{1,2,0:T(8,128)(2,1)}, u32[]{:S(2)}, u32[]{:S(2)}) collective-permute-start(bf16[2,256,512]{1,2,0:T(8,128)(2,1)} %pad_maximum_fusion.2), channel_id=1, source_target_pairs={{0,4},{4,8},{8,12},{12,16},{16,20},{20,24},{24,28},{1,5},{5,9},{9,... | collective-permute-start | bytes 1572872 | tf_op jit(solution)/shard_map/ppermute | solution.py:13
  20.4 0.9 compare_bitcast_fusion.1
  22.2 0.6 fusion.26
  23.2 0.5 copy-done.27
  24.6 1.5 select_convert_fusion.2
  26.8 0.6 copy-done.1
  28.3 1.1 fusion.66
  29.4 1.5 select_convert_fusion
  31.2 0.5 copy-done.2
  31.7 1.1 fusion.65
  32.8 1.5 select_convert_fusion.1
  34.7 0.5 copy-done.4
  35.5 0.8 multiply_convert_fusion
  36.4 0.5 fusion.30
  36.9 0.9 fusion.20
  38.0 0.9 copy-done.3
  38.9 1.0 fusion.70
  39.9 1.9 fusion.9
  41.9 0.6 fusion.8
  43.2 0.6 fusion.7
  43.8 2.1 copy.129
  46.2 0.4 fusion.34
  47.6 0.4 convolution_add_fusion.2
  48.1 1.2 fusion.16
  49.3 2.3 fusion.21
  51.6 1.0 fusion.68
  52.7 1.2 copy.121
  54.0 2.1 fusion.69
  56.1 2.0 copy.125
  58.1 1.0 convolution_multiply_fusion.7
  59.1 2.0 copy.124
  61.2 1.0 convolution_multiply_fusion.6
  62.2 2.0 copy.128
  64.2 2.3 pad_maximum_fusion.1
  66.6 1.3 collective-permute-start.3
  67.9 1.1 pad_maximum_fusion
  68.9 1.4 collective-permute-start.2
  71.0 0.6 copy-done.18
  72.0 0.8 copy.134
  73.2 111.2 %all-reduce.5.cloned.1.call-done = f32[4,128,128]{1,2,0:T(8,128)} async-done(((f32[4,128,128]{1,2,0:T(8,128)}), f32[4,128,128]{1,2,0:T(8,128)}) %all-reduce.5.cloned.1.call-update) | async-done | bytes 262160 | tf_op jit(solution)/shard_map/psum | solution.py:188
  184.5 1.8 copy.135
  186.3 1.8 fusion.19
  188.2 0.8 fusion.64
  189.0 67.1 %all-reduce.3.cloned.1.call-done = f32[128,512]{1,0:T(8,128)} async-done(((f32[128,512]{1,0:T(8,128)}), f32[128,512]{1,0:T(8,128)}) %all-reduce.3.cloned.1.call-update) | async-done | bytes 262160 | tf_op jit(solution)/shard_map/psum | solution.py:187
  256.1 1.7 copy.163
  (114 shorter events, 8.8 us)
Async XLA Ops:
  8.0 28.2 %copy-start = (bf16[512,512]{1,0:T(8,128)(2,1)S(1)}, bf16[512,512]{1,0:T(8,128)(2,1)}, u32[]{:S(2)}) copy-start(bf16[512,512]{1,0:T(8,128)(2,1)} %param.19) | copy-start | bytes 1572868
  8.0 1.2 copy-start.9
  8.0 176.5 %all-reduce.5.cloned.1.call-start = ((), (), s32[]{:S(2)}) async-start(), calls=%async_computation.3 | async-start | bytes 524288 | tf_op jit(solution)/shard_map/psum | solution.py:188
  10.2 18.1 %collective-permute-start.1 = (bf16[2,256,512]{1,2,0:T(8,128)(2,1)}, bf16[2,256,512]{1,2,0:T(8,128)(2,1)}, u32[]{:S(2)}, u32[]{:S(2)}) collective-permute-start(bf16[2,256,512]{1,2,0:T(8,128)(2,1)} %pad_maximum_fusion.2), channel_id=1, source_target_pairs={{0,8},{4,12},{8,16},{12,20},{16,24},{20,28},{1,9},{5,13},{9,17},{1... | collective-permute-start | bytes 1572872 | tf_op jit(solution)/shard_map/ppermute | solution.py:13
  16.0 15.7 %collective-permute-start = (bf16[2,256,512]{1,2,0:T(8,128)(2,1)}, bf16[2,256,512]{1,2,0:T(8,128)(2,1)}, u32[]{:S(2)}, u32[]{:S(2)}) collective-permute-start(bf16[2,256,512]{1,2,0:T(8,128)(2,1)} %pad_maximum_fusion.2), channel_id=1, source_target_pairs={{0,4},{4,8},{8,12},{12,16},{16,20},{20,24},{24,28},{1,5},{5,9},{9,... | collective-permute-start | bytes 1572872 | tf_op jit(solution)/shard_map/ppermute | solution.py:13
  20.2 1.6 copy-start.28
  20.3 5.8 %copy-start.7 = (bf16[256,4,128]{2,1,0:T(4,128)(2,1)}, bf16[256,4,128]{2,1,0:T(4,128)(2,1)S(1)}, u32[]{:S(2)}) copy-start(bf16[256,4,128]{2,1,0:T(4,128)(2,1)S(1)} %reshape_squeeze_stack_squeeze.9) | copy-start | bytes 786436
  20.3 2.7 %copy-start.19 = (bf16[1,256,512]{2,1,0:T(8,128)(2,1)S(1)}, bf16[1,256,512]{2,1,0:T(8,128)(2,1)}, u32[]{:S(2)}) copy-start(bf16[1,256,512]{2,1,0:T(8,128)(2,1)} %param.10) | copy-start | bytes 786436
  23.1 0.7 copy-start.27
  23.1 0.9 copy-start.20
  23.9 0.8 copy-start.25
  23.9 4.1 %copy-start.23 = (s32[1,256]{1,0:T(1,128)}, s32[1,256]{1,0:T(1,128)S(1)}, u32[]{:S(2)}) copy-start(s32[1,256]{1,0:T(1,128)S(1)} %get-tuple-element.40) | copy-start | bytes 3076
  26.5 1.0 copy-start.1
  27.4 2.0 copy-start.21
  29.4 1.5 copy-start.10
  29.4 1.5 copy-start.12
  30.9 0.8 copy-start.2
  32.8 1.5 copy-start.17
  32.8 1.5 copy-start.14
  34.3 0.8 copy-start.4
  35.4 1.0 copy-start.16
  37.8 1.0 copy-start.3
  38.9 1.0 copy-start.13
  38.9 1.0 copy-start.22
  39.9 1.9 copy-start.15
  39.9 1.9 copy-start.30
  41.8 1.0 copy-start.8
  41.9 1.3 copy-start.29
  43.8 2.1 copy-start.26
  46.2 0.7 copy-start.24
  49.3 137.0 %reduce-scatter.2.cloned.1.call-start = ((), (), s32[]{:S(2)}) async-start(), calls=%async_computation.1 | async-start | bytes 1310720 | tf_op jit(solution)/shard_map/reduce_scatter | solution.py:179
  53.9 202.1 %all-reduce.3.cloned.1.call-start = ((), (), s32[]{:S(2)}) async-start(), calls=%async_computation.2 | async-start | bytes 524288 | tf_op jit(solution)/shard_map/psum | solution.py:187
  64.2 3.6 %copy-start.5 = (f32[1,256,512]{2,1,0:T(8,128)S(1)}, f32[1,256,512]{2,1,0:T(8,128)}, u32[]{:S(2)}) copy-start(f32[1,256,512]{2,1,0:T(8,128)} %copy.125) | copy-start | bytes 1572868
  64.2 3.6 %copy-start.6 = (f32[1,256,512]{2,1,0:T(8,128)S(1)}, f32[1,256,512]{2,1,0:T(8,128)}, u32[]{:S(2)}) copy-start(f32[1,256,512]{2,1,0:T(8,128)} %copy.124) | copy-start | bytes 1572868
  66.6 119.8 %collective-permute-start.3 = (f32[2,256,512]{2,1,0:T(8,128)}, f32[2,256,512]{2,1,0:T(8,128)}, u32[]{:S(2)}, u32[]{:S(2)}) collective-permute-start(f32[2,256,512]{2,1,0:T(8,128)} %pad_maximum_fusion.1), channel_id=1, source_target_pairs={{8,0},{12,4},{16,8},{20,12},{24,16},{28,20},{9,1},{13,5},{17,9},{2... | collective-permute-start | bytes 3145736 | tf_op jit(solution)/shard_map/ppermute | solution.py:13
  68.9 1.7 copy-start.11
  68.9 117.4 %collective-permute-start.2 = (f32[2,256,512]{2,1,0:T(8,128)}, f32[2,256,512]{2,1,0:T(8,128)}, u32[]{:S(2)}, u32[]{:S(2)}) collective-permute-start(f32[2,256,512]{2,1,0:T(8,128)} %pad_maximum_fusion), channel_id=1, source_target_pairs={{4,0},{8,4},{12,8},{16,12},{20,16},{24,20},{28,24},{5,1},{9,5},{13... | collective-permute-start | bytes 3145736 | tf_op jit(solution)/shard_map/ppermute | solution.py:13
  70.7 1.0 copy-start.18
Sparse Core Ops, SparseCore 0:
  49.4 135.0 all-reduce.4
Sparse Core Ops, SparseCore 1:
  54.0 33.1 reduce-scatter.1
  186.4 69.6 all-reduce.2
where the time goes:
time: 266 us; the launch traced here: 265 us
  waiting for transfers between devices  178 us (67%)
  local copies, waits for them, and re-layouts  25 us (9%)
  matrix products  23.2 us (9%)
  between operations  16.1 us (6%)
  starting transfers between devices  12.8 us (5%)
  other arithmetic  9.79 us (4%)
    psum x1, waiting for transfers between devices, shards(): table_grad = lax.psum(table_local, ('ctx', 'dp'))  111 us
    psum x1, waiting for transfers between devices, shards(): projection_grad = lax.psum(weight_rows, 'ctx')  67.1 us
    ppermute x4, starting transfers between devices, passed_along(): return lax.ppermute(value, axis, pairs)  12.6 us
    unnamed x70, local copies, waits for them, and re-layouts  9.61 us
    another operation x3, local copies, waits for them, and re-layouts, shards(): key_terms.append(jnp.stack([key_part, value_part]))  5.33 us
  transfers between devices with their start and end apart: 7, of which 2 were waited for; matrix products, arithmetic and copies ran while one was open for 13% of the time, Pallas kernels for 0%

commit v1 on v0

--- a/solution.py
+++ b/solution.py
@@ -184,7 +184,7 @@
         scatter_dimension=0,
         tiled=True,
     )
-    projection_grad = lax.psum(weight_rows, "ctx")
+    projection_grad = jnp.sum(lax.all_gather(weight_rows, "ctx"), axis=0)
     table_grad = lax.psum(table_local, ("ctx", "dp"))
     return (
         query_grad[None],

time: 266 us -> 231 us (0.87)
  waiting for transfers between devices: 178 us -> 143 us
  local copies, waits for them, and re-layouts: 25 us -> 20.7 us
    psum x1 -> x0, waiting for transfers between devices: 67.1 us -> none  [shards(): projection_grad = lax.psum(weight_rows, 'ctx')]
    reduce_scatter x1, waiting for transfers between devices: 0.01 us -> 27.6 us  [shards(): lax.psum_scatter(lax.dot_general(mixed, grad_rows, (((0,), (0,)), ((), ()...]
    unnamed x70 -> x65, local copies, waits for them, and re-layouts: 9.61 us -> 4.71 us
    psum x1, waiting for transfers between devices: 111 us -> 115 us  [shards(): table_grad = lax.psum(table_local, ('ctx', 'dp'))]
  transfers between devices with their start and end apart: 7 -> 7, of which waited for: 2 -> 3; matrix products, arithmetic and copies ran while one was open for 13% -> 19% of each run, Pallas kernels for 0% -> 0%
where the time goes in v1:
time: 231 us; the launch traced here: 230 us
  waiting for transfers between devices  143 us (62%)
  matrix products  25.2 us (11%)
  local copies, waits for them, and re-layouts  20.7 us (9%)
  between operations  16.1 us (7%)
  starting transfers between devices  12.8 us (6%)
  other arithmetic  12.3 us (5%)
    psum x1, waiting for transfers between devices, shards(): table_grad = lax.psum(table_local, ('ctx', 'dp'))  115 us
    reduce_scatter x1, waiting for transfers between devices, shards(): lax.psum_scatter(lax.dot_general(mixed, grad_rows, (((0,), (0,)), ((), ()...  27.6 us
    ppermute x4, starting transfers between devices, passed_along(): return lax.ppermute(value, axis, pairs)  12.6 us
    another operation x3, local copies, waits for them, and re-layouts, shards(): key_terms.append(jnp.stack([key_part, value_part]))  5.33 us
    dot_general x3, matrix products, shards(): jnp.einsum('hij,ihd->jhd', weights, grad_heads, preferred_element_type=jn...  5.16 us
    unnamed x65, local copies, waits for them, and re-layouts  4.71 us
  transfers between devices with their start and end apart: 7, of which 3 were waited for; matrix products, arithmetic and copies ran while one was open for 19% of the time, Pallas kernels for 0%

profile of v1, /device:TPU:0, one launch (start us, length us, event | category | flops | bytes accessed | tf_op | source)
XLA Modules:
  0.0 229.9 jit_solution(11317034584292024249)
XLA Ops:
  8.1 1.2 copy.148
  9.3 1.1 copy.99
  10.4 0.8 pad_maximum_fusion.2
  11.2 5.8 %collective-permute-start.1 = (bf16[2,256,512]{1,2,0:T(8,128)(2,1)}, bf16[2,256,512]{1,2,0:T(8,128)(2,1)}, u32[]{:S(2)}, u32[]{:S(2)}) collective-permute-start(bf16[2,256,512]{1,2,0:T(8,128)(2,1)} %pad_maximum_fusion.2), channel_id=1, source_target_pairs={{0,8},{4,12},{8,16},{12,20},{16,24},{20,28},{1,9},{5,13},{9,17},{1... | collective-permute-start | bytes 1572872 | tf_op jit(solution)/shard_map/ppermute | solution.py:13
  17.0 4.2 %collective-permute-start = (bf16[2,256,512]{1,2,0:T(8,128)(2,1)}, bf16[2,256,512]{1,2,0:T(8,128)(2,1)}, u32[]{:S(2)}, u32[]{:S(2)}) collective-permute-start(bf16[2,256,512]{1,2,0:T(8,128)(2,1)} %pad_maximum_fusion.2), channel_id=1, source_target_pairs={{0,4},{4,8},{8,12},{12,16},{16,20},{20,24},{24,28},{1,5},{5,9},{9,... | collective-permute-start | bytes 1572872 | tf_op jit(solution)/shard_map/ppermute | solution.py:13
  21.3 0.9 compare_bitcast_fusion.1
  23.2 0.6 fusion.26
  24.9 1.4 select_convert_fusion.2
  26.7 0.8 copy.101
  27.7 0.4 fusion.49
  28.5 1.1 fusion.66
  29.6 1.6 select_convert_fusion
  31.6 1.1 fusion.65
  32.7 1.5 select_convert_fusion.1
  35.2 0.8 multiply_convert_fusion
  36.0 1.4 fusion.30
  37.4 0.9 fusion.20
  38.5 2.3 %fusion.21 = f32[512,512]{1,0:T(8,128)} fusion(bf16[256,512]{0,1:T(8,128)(2,1)} %bitcast.224, bf16[1,256,512]{2,1,0:T(8,128)(2,1)} %param.14), kind=kOutput, calls=%fused_computation.57 | convolution fusion | flops 134217728 | bytes 1572864 | tf_op jit(solution)/shard_map/dot_general | solution.py:180
  40.9 1.9 fusion.7
  42.9 0.4 fusion.38
  43.3 0.4 fusion.34
  43.8 0.6 fusion.8
  44.4 0.4 fusion.42
  45.1 0.6 fusion.9
  45.7 0.4 fusion.47
  46.0 0.4 convolution_add_fusion.2
  46.5 1.2 fusion.16
  47.7 27.6 %reduce-scatter.2.cloned.1.call-done = f32[128,512]{1,0:T(8,128)} async-done(((f32[512,512]{1,0:T(8,128)}), f32[128,512]{1,0:T(8,128)}) %reduce-scatter.2.cloned.1.call-update) | async-done | bytes 262160 | tf_op jit(solution)/shard_map/reduce_scatter | solution.py:179
  75.4 2.1 fusion.70
  77.4 2.0 copy.129
  79.5 1.0 fusion.68
  80.5 1.2 copy.121
  81.7 2.1 fusion.69
  83.8 2.1 copy.125
  85.9 1.0 convolution_multiply_fusion.7
  86.9 2.0 copy.124
  88.9 1.0 convolution_multiply_fusion.6
  90.0 2.0 copy.128
  92.0 2.4 %pad_maximum_fusion.1 = f32[2,256,512]{2,1,0:T(8,128)} fusion(f32[1,256,512]{2,1,0:T(8,128)} %copy.129, f32[1,256,512]{2,1,0:T(8,128)} %copy.128), kind=kLoop, calls=%fused_computation.41 | loop fusion | flops 262144 | bytes 2097152 | tf_op jit(solution)/shard_map/stack | solution.py:172
  94.4 1.4 collective-permute-start.3
  95.8 1.0 pad_maximum_fusion
  96.9 1.3 collective-permute-start.2
  99.1 0.8 copy.134
  100.4 115.1 %all-reduce.2.cloned.1.call-done = f32[4,128,128]{1,2,0:T(8,128)} async-done(((f32[4,128,128]{1,2,0:T(8,128)}), f32[4,128,128]{1,2,0:T(8,128)}) %all-reduce.2.cloned.1.call-update) | async-done | bytes 262160 | tf_op jit(solution)/shard_map/psum | solution.py:188
  215.5 1.8 copy.135
  217.3 1.8 fusion.19
  219.1 0.8 fusion.64
  220.0 2.5 %reduce_sum.83 = f32[128,512]{1,0:T(8,128)} reduce(f32[8,128,512]{2,1,0:T(8,128)} %bitcast.210, f32[]{:T(128)} %constant.165.clone.1), dimensions={0}, to_apply=%region_9.10 | reduce | flops 458752 | bytes 2359300 | tf_op jit(solution)/shard_map/reduce_sum | solution.py:187
  (110 shorter events, 6.5 us)
Async XLA Ops:
  8.0 28.0 %copy-start = (bf16[512,512]{1,0:T(8,128)(2,1)S(1)}, bf16[512,512]{1,0:T(8,128)(2,1)}, u32[]{:S(2)}) copy-start(bf16[512,512]{1,0:T(8,128)(2,1)} %param.19) | copy-start | bytes 1572868
  8.0 13.2 %copy-start.8 = (bf16[1,256,512]{2,1,0:T(8,128)(2,1)S(1)}, bf16[1,256,512]{2,1,0:T(8,128)(2,1)}, u32[]{:S(2)}) copy-start(bf16[1,256,512]{2,1,0:T(8,128)(2,1)} %param.12) | copy-start | bytes 786436
  8.0 14.8 %copy-start.26 = (s32[1,6]{1,0:T(1,128)S(1)}, s32[1,6]{1,0:T(1,128)}, u32[]{:S(2)}) copy-start(s32[1,6]{1,0:T(1,128)} %param.16) | copy-start | bytes 76
  8.0 16.0 %copy-start.17 = (bf16[1,256,512]{2,1,0:T(8,128)(2,1)S(1)}, bf16[1,256,512]{2,1,0:T(8,128)(2,1)}, u32[]{:S(2)}) copy-start(bf16[1,256,512]{2,1,0:T(8,128)(2,1)} %param.10) | copy-start | bytes 786436
  8.0 16.1 %copy-start.25 = (s32[1,2048]{1,0:T(1,128)S(1)}, s32[1,2048]{1,0:T(1,128)}, u32[]{:S(2)}) copy-start(s32[1,2048]{1,0:T(1,128)} %param.15) | copy-start | bytes 24580
  8.1 16.2 %copy-start.18 = (bf16[4,128,128]{2,1,0:T(8,128)(2,1)S(1)}, bf16[4,128,128]{2,1,0:T(8,128)(2,1)}, u32[]{:S(2)}) copy-start(bf16[4,128,128]{2,1,0:T(8,128)(2,1)} %param.18) | copy-start | bytes 393220
  8.1 67.3 %reduce-scatter.2.cloned.1.call-start = ((), (), s32[]{:S(2)}) async-start(), calls=%async_computation.1 | async-start | bytes 1310720 | tf_op jit(solution)/shard_map/reduce_scatter | solution.py:179
  11.2 17.3 %collective-permute-start.1 = (bf16[2,256,512]{1,2,0:T(8,128)(2,1)}, bf16[2,256,512]{1,2,0:T(8,128)(2,1)}, u32[]{:S(2)}, u32[]{:S(2)}) collective-permute-start(bf16[2,256,512]{1,2,0:T(8,128)(2,1)} %pad_maximum_fusion.2), channel_id=1, source_target_pairs={{0,8},{4,12},{8,16},{12,20},{16,24},{20,28},{1,9},{5,13},{9,17},{1... | collective-permute-start | bytes 1572872 | tf_op jit(solution)/shard_map/ppermute | solution.py:13
  17.0 14.6 %collective-permute-start = (bf16[2,256,512]{1,2,0:T(8,128)(2,1)}, bf16[2,256,512]{1,2,0:T(8,128)(2,1)}, u32[]{:S(2)}, u32[]{:S(2)}) collective-permute-start(bf16[2,256,512]{1,2,0:T(8,128)(2,1)} %pad_maximum_fusion.2), channel_id=1, source_target_pairs={{0,4},{4,8},{8,12},{12,16},{16,20},{20,24},{24,28},{1,5},{5,9},{9,... | collective-permute-start | bytes 1572872 | tf_op jit(solution)/shard_map/ppermute | solution.py:13
  21.3 5.0 %copy-start.6 = (bf16[256,4,128]{2,1,0:T(4,128)(2,1)}, bf16[256,4,128]{2,1,0:T(4,128)(2,1)S(1)}, u32[]{:S(2)}) copy-start(bf16[256,4,128]{2,1,0:T(4,128)(2,1)S(1)} %reshape_squeeze_stack_squeeze.9) | copy-start | bytes 786436
  24.2 2.1 copy-start.23
  24.2 3.9 %copy-start.21 = (s32[1,256]{1,0:T(1,128)}, s32[1,256]{1,0:T(1,128)S(1)}, u32[]{:S(2)}) copy-start(s32[1,256]{1,0:T(1,128)S(1)} %get-tuple-element.40) | copy-start | bytes 3076
  24.9 2.7 %copy-start.1 = (bf16[1,256,512]{2,1,0:T(8,128)(2,1)S(1)}, bf16[1,256,512]{2,1,0:T(8,128)(2,1)}, u32[]{:S(2)}) copy-start(bf16[1,256,512]{2,1,0:T(8,128)(2,1)} %param.13) | copy-start | bytes 786436
  29.6 1.6 copy-start.9
  29.6 1.6 copy-start.11
  31.1 3.0 %copy-start.2 = (bf16[4,256,256]{2,1,0:T(8,128)(2,1)}, bf16[4,256,256]{2,1,0:T(8,128)(2,1)S(1)}, u32[]{:S(2)}) copy-start(bf16[4,256,256]{2,1,0:T(8,128)(2,1)S(1)} %get-tuple-element.47) | copy-start | bytes 1572868
  31.1 1.5 copy-start.19
  32.6 1.5 copy-start.15
  32.7 1.5 copy-start.13
  34.2 0.8 copy-start.3
  37.4 3.5 %copy-start.7 = (bf16[256,4,128]{2,1,0:T(4,128)(2,1)S(1)}, bf16[256,4,128]{2,1,0:T(4,128)(2,1)}, u32[]{:S(2)}) copy-start(bf16[256,4,128]{2,1,0:T(4,128)(2,1)} %copy-done.6) | copy-start | bytes 786436
  40.8 174.7 %all-reduce.2.cloned.1.call-start = ((), (), s32[]{:S(2)}) async-start(), calls=%async_computation.2 | async-start | bytes 524288 | tf_op jit(solution)/shard_map/psum | solution.py:188
  40.9 2.0 copy-start.24
  40.9 2.8 %copy-start.14 = (bf16[1,256,512]{1,2,0:T(8,128)(2,1)S(1)}, bf16[1,256,512]{1,2,0:T(8,128)(2,1)}, u32[]{:S(2)}) copy-start(bf16[1,256,512]{1,2,0:T(8,128)(2,1)} %copy-done.13) | copy-start | bytes 786436
  40.9 2.8 %copy-start.20 = (pred[256,256]{1,0:T(8,128)(4,1)S(1)}, pred[256,256]{1,0:T(8,128)(4,1)}, u32[]{:S(2)}) copy-start(pred[256,256]{1,0:T(8,128)(4,1)} %copy.101) | copy-start | bytes 196612
  40.9 2.8 %copy-start.28 = (f32[4,256,256]{2,1,0:T(8,128)S(1)}, f32[4,256,256]{2,1,0:T(8,128)}, u32[]{:S(2)}) copy-start(f32[4,256,256]{2,1,0:T(8,128)} %get-tuple-element.52) | copy-start | bytes 3145732
  43.7 0.6 copy-start.22
  43.7 1.0 copy-start.12
  43.8 1.3 copy-start.27
  47.7 172.3 %all-gather.3.cloned.1.call-start = ((), (), s32[]{:S(2)}) async-start(), calls=%async_computation.3 | async-start | bytes 2359296 | tf_op jit(solution)/shard_map/all_gather | solution.py:187
  92.0 3.8 %copy-start.4 = (f32[1,256,512]{2,1,0:T(8,128)S(1)}, f32[1,256,512]{2,1,0:T(8,128)}, u32[]{:S(2)}) copy-start(f32[1,256,512]{2,1,0:T(8,128)} %copy.125) | copy-start | bytes 1572868
  92.0 3.8 %copy-start.5 = (f32[1,256,512]{2,1,0:T(8,128)S(1)}, f32[1,256,512]{2,1,0:T(8,128)}, u32[]{:S(2)}) copy-start(f32[1,256,512]{2,1,0:T(8,128)} %copy.124) | copy-start | bytes 1572868
  94.4 4.1 %copy-start.10 = (bf16[1,256,512]{1,2,0:T(8,128)(2,1)S(1)}, bf16[1,256,512]{1,2,0:T(8,128)(2,1)}, u32[]{:S(2)}) copy-start(bf16[1,256,512]{1,2,0:T(8,128)(2,1)} %copy-done.9) | copy-start | bytes 786436
  94.4 4.4 %copy-start.16 = (bf16[1,256,512]{1,2,0:T(8,128)(2,1)S(1)}, bf16[1,256,512]{1,2,0:T(8,128)(2,1)}, u32[]{:S(2)}) copy-start(bf16[1,256,512]{1,2,0:T(8,128)(2,1)} %copy-done.15) | copy-start | bytes 786436
  94.4 122.9 %collective-permute-start.3 = (f32[2,256,512]{2,1,0:T(8,128)}, f32[2,256,512]{2,1,0:T(8,128)}, u32[]{:S(2)}, u32[]{:S(2)}) collective-permute-start(f32[2,256,512]{2,1,0:T(8,128)} %pad_maximum_fusion.1), channel_id=1, source_target_pairs={{8,0},{12,4},{16,8},{20,12},{24,16},{28,20},{9,1},{13,5},{17,9},{2... | collective-permute-start | bytes 3145736 | tf_op jit(solution)/shard_map/ppermute | solution.py:13
  96.9 120.4 %collective-permute-start.2 = (f32[2,256,512]{2,1,0:T(8,128)}, f32[2,256,512]{2,1,0:T(8,128)}, u32[]{:S(2)}, u32[]{:S(2)}) collective-permute-start(f32[2,256,512]{2,1,0:T(8,128)} %pad_maximum_fusion), channel_id=1, source_target_pairs={{4,0},{8,4},{12,8},{16,12},{20,16},{24,20},{28,24},{5,1},{9,5},{13... | collective-permute-start | bytes 3145736 | tf_op jit(solution)/shard_map/ppermute | solution.py:13
Sparse Core Ops, SparseCore 0:
  40.9 34.3 reduce-scatter.1
  77.5 63.5 all-gather.2
Sparse Core Ops, SparseCore 1:
  47.8 167.7 all-reduce.1
